TPU v7x, 128 devices: a whole 4x4x4 slice. The times are simulated.
128 devices in a mesh: dp: 16 (over x, y_lo, core), tensor: 8 (over z, y_hi).
Axes of the slice: x: 4, y: 4 (y_hi: 2, y_lo: 2; y = y_hi * 2 + y_lo), z: 4, core: 2. Of those that a mesh axis runs over, the one named last changes fastest.
Arguments:
- rows_in: bfloat16 [2048, 6144], P('dp'), may hold values from -6 to 6
- out_grad: bfloat16 [2048, 6144], P('dp'), may hold values from -1.5 to 1.5
- gate_pre: bfloat16 [2048, 12288], P('dp', 'tensor'), may hold values from -5 to 5
- up_pre: bfloat16 [2048, 12288], P('dp', 'tensor'), may hold values from -5 to 5
- w_gate: bfloat16 [2, 6144, 12288], P(None, 'dp', 'tensor'), may hold values from -0.078125 to 0.078125
- w_up: bfloat16 [2, 6144, 12288], P(None, 'dp', 'tensor'), may hold values from -0.078125 to 0.078125
- w_down: bfloat16 [2, 12288, 6144], P(None, 'tensor', 'dp'), may hold values from -0.0546875 to 0.0546875
- live_rows: int32 [16], P('dp'), may hold values from 32 to 128, as said below
- block_expert: int32 [16], replicated, may hold values from 0 to 1, as said below
Outputs:
- input_grad: bfloat16 [2048, 6144], P('dp', 'tensor')
- grad_gate: bfloat16 [2, 6144, 12288], P(None, 'dp', 'tensor')
- grad_up: bfloat16 [2, 6144, 12288], P(None, 'dp', 'tensor')
- grad_down: bfloat16 [2, 12288, 6144], P(None, 'tensor', 'dp')
Inputs may be any that keep to these rules, and one draw needn't show every extreme that they name: `live_rows`: entry k counts the live rows among rank k's 128 rows; they come first and the rest are padding; some rank is full. `block_expert`: the expert of each aligned block of 128 rows; every expert owns at least one block.
All inputs are finite; a program needn't handle non-finite values.
Results may differ from a plain program's by a relative error of at most 0.005.
Values may be sent and summed in bfloat16 or wider, within the bound.
No kernel may reach another device: no remote copies, remote signals or barrier semaphores. Data moves between devices by JAX's collectives and lax.ppermute only.
A program may use at most 128 MiB of HBM per device.

v0:
```python
import numpy as np
import jax
import jax.numpy as jnp
from jax import lax
from jax.sharding import Mesh
from jax.sharding import PartitionSpec as P

BLOCK = 128
AXES = ("x", "ylo", "core", "z", "yhi")
SIZES = (4, 2, 2, 4, 2)
DP = ("x", "ylo", "core")
TP = ("z", "yhi")
CHIPS = ("x", "ylo")
N_DP = 16
N_TP = 8


def rank_of_pos(pos):
    core, x, ylo = (pos // 8, pos % 8 // 2, pos % 2)
    return x * 4 + ylo * 2 + core


POS_RANK = np.array([rank_of_pos(p) for p in range(N_DP)], np.int32)


def deliver_perm(k):
    pairs = []
    for i in range(N_DP):
        for t in range(N_TP):
            dest = 8 * (i % 2 ^ k) + t
            pairs.append((i * N_TP + t, dest * N_TP + i // 2))
    return pairs


def contract_rows(left_op, right_op):
    return lax.dot_general(
        left_op, right_op, (((0,), (0,)), ((), ())), preferred_element_type=jnp.float32
    )


def contract_cols(left_op, right_op):
    return lax.dot_general(
        left_op, right_op, (((1,), (1,)), ((), ())), preferred_element_type=jnp.float32
    )


def expert_masks(block_expert, row_count, expert_count):
    spread = jnp.broadcast_to(block_expert[:, None], (row_count // BLOCK, BLOCK)).reshape(
        row_count, 1
    )
    return [(spread == which).astype(jnp.bfloat16) for which in range(expert_count)]


def to_gathered_order(cols):
    width = cols.shape[1]
    return cols.reshape(4, 2, 2, BLOCK, width).transpose(2, 0, 1, 3, 4).reshape(-1, width)


def shards(rows_in, out_grad, gate_pre, up_pre, w_gate, w_up, w_down, live_rows, block_expert):
    rows_dev = rows_in.shape[0]
    expert_count = w_gate.shape[0]
    ff = gate_pre.shape[1]
    dy_cols = lax.all_to_all(out_grad, DP, split_axis=1, concat_axis=0, tiled=True)
    row_count = dy_cols.shape[0]
    expert_g = jnp.take(block_expert, jnp.asarray(POS_RANK), axis=0)
    masks_g = expert_masks(expert_g, row_count, expert_count)
    masks = expert_masks(block_expert, row_count, expert_count)
    positions = jnp.arange(rows_dev, dtype=jnp.int32)[:, None]
    row_mask = (positions < live_rows[0]).astype(jnp.float32)
    gate_vals = gate_pre.astype(jnp.float32)
    up_vals = up_pre.astype(jnp.float32)
    sigmoid = jax.nn.sigmoid(gate_vals)
    silu_vals = gate_vals * sigmoid
    hidden = (silu_vals * up_vals * row_mask).astype(jnp.bfloat16)
    hid_g = lax.all_gather(hidden, DP, axis=0, tiled=True)
    dy_g = to_gathered_order(dy_cols)
    result = jnp.zeros((row_count, ff), jnp.float32)
    for which in range(expert_count):
        result = result + contract_cols(dy_g * masks_g[which], w_down[which])
    hid_g, result = lax.optimization_barrier((hid_g, result))
    result = lax.psum_scatter(
        result.reshape(2, row_count // 2, ff), "core", scatter_dimension=0, tiled=True
    ).reshape(N_DP // 2, rows_dev, ff)
    pieces = lax.all_to_all(result, CHIPS, split_axis=0, concat_axis=0, tiled=True)
    hidden_grad = jnp.sum(pieces, axis=0)
    rows_in, hidden_grad = lax.optimization_barrier((rows_in, hidden_grad))
    x_cols = lax.all_to_all(rows_in, DP, split_axis=1, concat_axis=0, tiled=True)
    up_grad = (hidden_grad * silu_vals * row_mask).astype(jnp.bfloat16)
    gate_grad = (
        hidden_grad * up_vals * sigmoid * (1.0 + gate_vals * (1.0 - sigmoid)) * row_mask
    ).astype(jnp.bfloat16)
    packed = jnp.stack([gate_grad, up_grad], axis=1)
    packed = lax.all_gather(packed, DP, axis=0, tiled=True)
    gate_g, up_g = (packed[:, 0], packed[:, 1])
    down_terms = []
    gate_terms = []
    up_terms = []
    for which in range(expert_count):
        down_terms.append(contract_rows(hid_g * masks[which], dy_cols))
        gate_masked = gate_g * masks[which]
        up_masked = up_g * masks[which]
        gate_terms.append(contract_rows(x_cols, gate_masked))
        up_terms.append(contract_rows(x_cols, up_masked))
    down_total = jnp.stack(down_terms, 0)
    gate_total = jnp.stack(gate_terms, 0)
    up_total = jnp.stack(up_terms, 0)
    width = w_gate.shape[1]
    half_rows = row_count // 2
    summed = []
    for half in range(2):
        rows = slice(half * half_rows, (half + 1) * half_rows)
        partial_rows = jnp.zeros((half_rows, width), jnp.float32)
        for which in range(expert_count):
            gate_masked = gate_g[rows] * masks[which][rows]
            up_masked = up_g[rows] * masks[which][rows]
            partial_rows = (
                partial_rows
                + contract_cols(gate_masked, w_gate[which])
                + contract_cols(up_masked, w_up[which])
            )
        pieces = lax.all_to_all(
            partial_rows.reshape(N_TP, rows_dev, width), TP, split_axis=0, concat_axis=0, tiled=True
        )
        summed.append(jnp.sum(pieces, axis=0))
    summed = jnp.stack(summed, 0)
    core = lax.axis_index("core")
    low = lax.axis_index("x") < 2
    got = []
    for k in range(2):
        piece = lax.dynamic_index_in_dim(summed, core ^ k, 0, keepdims=False)
        got.append(lax.ppermute(piece, AXES, deliver_perm(k)))
    first = jnp.where(low, got[0], got[1])
    second = jnp.where(low, got[1], got[0])
    input_grad = jnp.concatenate([first, second], axis=1).astype(jnp.bfloat16)
    return (
        input_grad,
        gate_total.astype(jnp.bfloat16),
        up_total.astype(jnp.bfloat16),
        down_total.astype(jnp.bfloat16),
    )


def solution(mesh):
    fine = Mesh(mesh.devices.reshape(SIZES), AXES)
    return jax.shard_map(
        shards,
        mesh=fine,
        in_specs=(
            P(DP, None),
            P(DP, None),
            P(DP, TP),
            P(DP, TP),
            P(None, DP, TP),
            P(None, DP, TP),
            P(None, TP, DP),
            P(DP),
            P(),
        ),
        out_specs=(P(DP, TP), P(None, DP, TP), P(None, DP, TP), P(None, TP, DP)),
        check_vma=False,
    )
```

profile of v0, /device:TPU:3, one launch (start us, length us, event | category | flops | bytes accessed | tf_op | source)
XLA Modules:
  0.0 359.7 jit_solution(13972185572916459537)
XLA Ops:
  11.7 6.3 %all-to-all-start = ((bf16[128,16,384]{0,2,1:T(8,128)(2,1)}), bf16[128,16,384]{0,2,1:T(8,128)(2,1)S(1)}, u32[]{:S(2)}, u32[]{:S(2)}) async-start(bf16[128,16,384]{0,2,1:T(8,128)(2,1)} %bitcast.1), calls=%async_computation | async-start | bytes 3145728 | tf_op jit(solution)/shard_map/all_to_all | solution.py:63
  19.2 30.3 %all-to-all-done = bf16[128,16,384]{0,2,1:T(8,128)(2,1)S(1)} async-done(((bf16[128,16,384]{0,2,1:T(8,128)(2,1)}), bf16[128,16,384]{0,2,1:T(8,128)(2,1)S(1)}, u32[]{:S(2)}, u32[]{:S(2)}) %all-to-all-start) | async-done | bytes 1572896 | tf_op jit(solution)/shard_map/all_to_all | solution.py:63
  52.7 3.5 fusion.115
  56.1 6.7 %convolution_add_fusion = f32[2048,1536]{1,0:T(8,128)} fusion(f32[2048,1536]{1,0:T(8,128)S(1)} %fusion.115, bf16[2048,384]{1,0:T(8,128)(2,1)S(1)} %bitcast.142, bf16[2,1536,384]{2,1,0:T(8,128)(2,1)S(1)} %copy-done.1), kind=kOutput, calls=%fused_computation.1 | convolution fusion | flops 2419064832 | bytes 27918336 | tf_op jit(solution)/shard_map/dot_general | solution.py:42
  62.8 6.6 %all-gather.3.cloned.1.call-done = bf16[2048,1536]{1,0:T(8,128)(2,1)} async-done(((bf16[128,1536]{1,0:T(8,128)(2,1)}), bf16[2048,1536]{1,0:T(8,128)(2,1)}) %all-gather.3.cloned.1.call-update) | async-done | bytes 6291472 | tf_op jit(solution)/shard_map/all_gather | solution.py:75
  69.5 28.4 %reduce-scatter.2.cloned.1.call-done = f32[1,1024,1536]{2,1,0:T(8,128)} async-done(((f32[2,1024,1536]{2,1,0:T(8,128)}), f32[1,1024,1536]{2,1,0:T(8,128)}) %reduce-scatter.2.cloned.1.call-update) | async-done | bytes 6291472 | tf_op jit(solution)/shard_map/reduce_scatter | solution.py:81
  97.9 75.3 %all_to_all.53 = f32[8,128,1536]{2,1,0:T(8,128)} all-to-all(f32[8,128,1536]{2,1,0:T(8,128)} %bitcast.144), channel_id=1, replica_groups=mesh['x'=4,'ylo'=2,'core'=2,'z'=4,'yhi'=2] {'x','ylo'}, dimensions={0} | all-to-all | bytes 12582912 | tf_op jit(solution)/shard_map/all_to_all | solution.py:84
  173.2 3.4 reduce_sum.27
  180.4 6.1 %all-to-all-start.4 = ((bf16[128,16,384]{0,2,1:T(8,128)(2,1)}), bf16[128,16,384]{0,2,1:T(8,128)(2,1)S(1)}, u32[]{:S(2)}, u32[]{:S(2)}) async-start(bf16[128,16,384]{0,2,1:T(8,128)(2,1)} %bitcast.36), calls=%async_computation.5 | async-start | bytes 3145728 | tf_op jit(solution)/shard_map/all_to_all | solution.py:87
  186.5 6.3 %fusion.88 = bf16[1,1536,384]{2,1,0:T(8,128)(2,1)S(1)} fusion(bf16[2048,384]{1,0:T(8,128)(2,1)S(1)} %bitcast.148, bf16[2048,1536]{1,0:T(8,128)(2,1)} %all-gather.3.cloned.1.call-done, bf16[2048]{0:T(1024)(128)(2,1)S(1)} %broadcast_bitcast_fusion), kind=kOutput, calls=%fused_computation.70 | convolution fusion | flops 2419654656 | bytes 9048064 | tf_op jit(solution)/shard_map/dot_general | solution.py:36
  192.8 6.3 %fusion.91 = bf16[1,1536,384]{2,1,0:T(8,128)(2,1)S(1)} fusion(bf16[2048,384]{1,0:T(8,128)(2,1)S(1)} %bitcast.149, bf16[2048,1536]{1,0:T(8,128)(2,1)} %all-gather.3.cloned.1.call-done, bf16[2048]{0:T(1024)(128)(2,1)S(1)} %broadcast_bitcast_fusion.1), kind=kOutput, calls=%fused_computation.71 | convolution fusion | flops 2419654656 | bytes 9048064 | tf_op jit(solution)/shard_map/dot_general | solution.py:36
  200.8 18.7 %all-to-all-done.4 = bf16[128,16,384]{0,2,1:T(8,128)(2,1)S(1)} async-done(((bf16[128,16,384]{0,2,1:T(8,128)(2,1)}), bf16[128,16,384]{0,2,1:T(8,128)(2,1)S(1)}, u32[]{:S(2)}, u32[]{:S(2)}) %all-to-all-start.4) | async-done | bytes 1572896 | tf_op jit(solution)/shard_map/all_to_all | solution.py:87
  221.1 45.7 %all-gather.5.cloned.1.call-done = bf16[2048,2,1536]{2,0,1:T(8,128)(2,1)} async-done(((bf16[128,2,1536]{2,0,1:T(8,128)(2,1)}), bf16[2048,2,1536]{2,0,1:T(8,128)(2,1)}) %all-gather.5.cloned.1.call-update) | async-done | bytes 12582928 | tf_op jit(solution)/shard_map/all_gather | solution.py:93
  266.8 4.2 %fusion.20 = f32[1024,384]{1,0:T(8,128)S(1)} fusion(bf16[2048,2,1536]{2,0,1:T(8,128)(2,1)} %all-gather.5.cloned.1.call-done, bf16[1024]{0:T(1024)(128)(2,1)S(1)} %broadcast_bitcast_fusion.2, bf16[2,384,1536]{2,1,0:T(8,128)(2,1)} %param.15), kind=kOutput, calls=%fused_computation.22 | convolution fusion | flops 1209532416 | bytes 5900288 | tf_op jit(solution)/shard_map/dot_general | solution.py:42
  279.3 6.8 %all-to-all-start.3 = ((f32[8,128,384]{2,1,0:T(8,128)}), f32[8,128,384]{2,1,0:T(8,128)S(1)}, u32[]{:S(2)}, u32[]{:S(2)}) async-start(f32[8,128,384]{2,1,0:T(8,128)} %bitcast.32), calls=%async_computation.4 | async-start | bytes 3145728 | tf_op jit(solution)/shard_map/all_to_all | solution.py:121
  286.1 4.2 %fusion.32 = f32[1024,384]{1,0:T(8,128)S(1)} fusion(bf16[2048,2,1536]{2,0,1:T(8,128)(2,1)} %all-gather.5.cloned.1.call-done, bf16[1024]{0:T(1024)(128)(2,1)S(1)} %broadcast_bitcast_fusion.5, bf16[2,384,1536]{2,1,0:T(8,128)(2,1)} %param.15), kind=kOutput, calls=%fused_computation.34 | convolution fusion | flops 1209532416 | bytes 5900288 | tf_op jit(solution)/shard_map/dot_general | solution.py:42
  290.3 3.9 %fusion.34 = f32[1024,384]{1,0:T(8,128)S(1)} fusion(bf16[2048,2,1536]{2,0,1:T(8,128)(2,1)} %all-gather.5.cloned.1.call-done, bf16[1024]{0:T(1024)(128)(2,1)S(1)} %broadcast_bitcast_fusion.5, bf16[2,384,1536]{2,1,0:T(8,128)(2,1)S(1)} %copy-done.14), kind=kOutput, calls=%fused_computation.36 | convolution fusion | flops 1209532416 | bytes 5900288 | tf_op jit(solution)/shard_map/dot_general | solution.py:42
  304.1 3.1 add_add_fusion.1
  308.4 5.4 %all-to-all-start.2 = ((f32[8,128,384]{2,1,0:T(8,128)}), f32[8,128,384]{2,1,0:T(8,128)S(1)}, u32[]{:S(2)}, u32[]{:S(2)}) async-start(f32[8,128,384]{2,1,0:T(8,128)} %bitcast.154), calls=%async_computation.3 | async-start | bytes 3145728 | tf_op jit(solution)/shard_map/all_to_all | solution.py:121
  313.9 7.1 %fusion.76 = bf16[1,384,1536]{2,1,0:T(8,128)(2,1)} fusion(bf16[2048,384]{1,0:T(8,128)(2,1)} %bitcast.150, bf16[2048,2,1536]{2,0,1:T(8,128)(2,1)} %all-gather.5.cloned.1.call-done, bf16[2048]{0:T(1024)(128)(2,1)S(1)} %broadcast_bitcast_fusion), kind=kOutput, calls=%fused_computation.66 | convolution fusion | flops 2419654656 | bytes 9048064 | tf_op jit(solution)/shard_map/dot_general | solution.py:36
  321.0 6.5 %fusion.79 = bf16[1,384,1536]{2,1,0:T(8,128)(2,1)} fusion(bf16[2048,384]{1,0:T(8,128)(2,1)S(1)} %bitcast.153, bf16[2048,2,1536]{2,0,1:T(8,128)(2,1)} %all-gather.5.cloned.1.call-done, bf16[2048]{0:T(1024)(128)(2,1)S(1)} %broadcast_bitcast_fusion.1), kind=kOutput, calls=%fused_computation.67 | convolution fusion | flops 2419654656 | bytes 9048064 | tf_op jit(solution)/shard_map/dot_general | solution.py:36
  327.6 8.1 %all-to-all-done.2 = f32[8,128,384]{2,1,0:T(8,128)S(1)} async-done(((f32[8,128,384]{2,1,0:T(8,128)}), f32[8,128,384]{2,1,0:T(8,128)S(1)}, u32[]{:S(2)}, u32[]{:S(2)}) %all-to-all-start.2) | async-done | bytes 1572896 | tf_op jit(solution)/shard_map/all_to_all | solution.py:121
  335.8 3.6 collective-permute-start
  344.9 4.6 %collective-permute-done = bf16[128,384]{1,0:T(8,128)(2,1)S(1)} collective-permute-done((bf16[128,384]{1,0:T(8,128)(2,1)S(1)}, bf16[128,384]{1,0:T(8,128)(2,1)S(1)}, u32[]{:S(2)}, u32[]{:S(2)}) %collective-permute-start) | collective-permute-done | bytes 98336 | tf_op jit(solution)/shard_map/ppermute | solution.py:131
  (86 shorter events, 43.8 us)
Async XLA Ops:
  7.2 3.0 copy-start.2
  7.2 62.3 %all-gather.3.cloned.1.call-start = ((), (), s32[]{:S(2)}) async-start(), calls=%async_computation.6 | async-start | bytes 6684672 | tf_op jit(solution)/shard_map/all_gather | solution.py:75
  11.7 6.4 %copy-start.9 = (s32[16]{0:T(128)S(1)}, s32[16]{0:T(128)}, u32[]{:S(2)}) copy-start(s32[16]{0:T(128)} %constant.55) | copy-start | bytes 196
  11.7 6.4 %copy-start = (s32[16]{0:T(128)S(1)}, s32[16]{0:T(128)}, u32[]{:S(2)}) copy-start(s32[16]{0:T(128)} %param.18) | copy-start | bytes 196
  11.7 37.8 %all-to-all-start = ((bf16[128,16,384]{0,2,1:T(8,128)(2,1)}), bf16[128,16,384]{0,2,1:T(8,128)(2,1)S(1)}, u32[]{:S(2)}, u32[]{:S(2)}) async-start(bf16[128,16,384]{0,2,1:T(8,128)(2,1)} %bitcast.1), calls=%async_computation | async-start | bytes 3145728 | tf_op jit(solution)/shard_map/all_to_all | solution.py:63
  18.0 79.9 %reduce-scatter.2.cloned.1.call-start = ((), (), s32[]{:S(2)}) async-start(), calls=%async_computation.7 | async-start | bytes 18874368 | tf_op jit(solution)/shard_map/reduce_scatter | solution.py:81
  69.5 197.3 %all-gather.5.cloned.1.call-start = ((), (), s32[]{:S(2)}) async-start(), calls=%async_computation.8 | async-start | bytes 13369344 | tf_op jit(solution)/shard_map/all_gather | solution.py:93
  173.2 3.4 copy-start.6
  173.2 3.4 copy-start.7
  180.4 39.1 %all-to-all-start.4 = ((bf16[128,16,384]{0,2,1:T(8,128)(2,1)}), bf16[128,16,384]{0,2,1:T(8,128)(2,1)S(1)}, u32[]{:S(2)}, u32[]{:S(2)}) async-start(bf16[128,16,384]{0,2,1:T(8,128)(2,1)} %bitcast.36), calls=%async_computation.5 | async-start | bytes 3145728 | tf_op jit(solution)/shard_map/all_to_all | solution.py:87
  221.1 49.9 %copy-start.11 = (bf16[2,384,1536]{2,1,0:T(8,128)(2,1)S(1)}, bf16[2,384,1536]{2,1,0:T(8,128)(2,1)}, u32[]{:S(2)}) copy-start(bf16[2,384,1536]{2,1,0:T(8,128)(2,1)} %param.15) | copy-start | bytes 7077892
  266.8 5.9 %copy-start.10 = (bf16[2048,2,1536]{2,0,1:T(8,128)(2,1)S(1)}, bf16[2048,2,1536]{2,0,1:T(8,128)(2,1)}, u32[]{:S(2)}) copy-start(bf16[2048,2,1536]{2,0,1:T(8,128)(2,1)} %all-gather.5.cloned.1.call-done) | copy-start | bytes 37748740
  279.3 29.1 %all-to-all-start.3 = ((f32[8,128,384]{2,1,0:T(8,128)}), f32[8,128,384]{2,1,0:T(8,128)S(1)}, u32[]{:S(2)}, u32[]{:S(2)}) async-start(f32[8,128,384]{2,1,0:T(8,128)} %bitcast.32), calls=%async_computation.4 | async-start | bytes 3145728 | tf_op jit(solution)/shard_map/all_to_all | solution.py:121
  286.1 4.2 %copy-start.14 = (bf16[2,384,1536]{2,1,0:T(8,128)(2,1)S(1)}, bf16[2,384,1536]{2,1,0:T(8,128)(2,1)}, u32[]{:S(2)}) copy-start(bf16[2,384,1536]{2,1,0:T(8,128)(2,1)} %param.14) | copy-start | bytes 7077892
  286.1 8.2 %slice-start = ((s8[12582912]{0:T(1024)(128)(4,1)}), s8[4194304]{0:T(1024)(128)(4,1)S(1)}, s32[]{:S(2)}) async-start(s8[12582912]{0:T(1024)(128)(4,1)} %bitcast.157), calls=%async_computation.9 | async-start | bytes 8388608
  286.1 8.2 %slice-start.1 = ((s8[12582912]{0:T(1024)(128)(4,1)}), s8[4194304]{0:T(1024)(128)(4,1)S(1)}, s32[]{:S(2)}) async-start(s8[12582912]{0:T(1024)(128)(4,1)} %bitcast.157), calls=%async_computation.10 | async-start | bytes 8388608
  290.3 3.9 %copy-start.4 = (bf16[16,128,384]{2,1,0:T(8,128)(2,1)S(1)}, bf16[16,128,384]{2,1,0:T(8,128)(2,1)}, u32[]{:S(2)}) copy-start(bf16[16,128,384]{2,1,0:T(8,128)(2,1)} %copy.23) | copy-start | bytes 4718596
  290.3 4.0 %slice-start.2 = ((s8[12582912]{0:T(1024)(128)(4,1)}), s8[4194304]{0:T(1024)(128)(4,1)S(1)}, s32[]{:S(2)}) async-start(s8[12582912]{0:T(1024)(128)(4,1)} %bitcast.157), calls=%async_computation.11 | async-start | bytes 8388608
  299.8 2.5 copy-start.12
  308.4 27.2 %all-to-all-start.2 = ((f32[8,128,384]{2,1,0:T(8,128)}), f32[8,128,384]{2,1,0:T(8,128)S(1)}, u32[]{:S(2)}, u32[]{:S(2)}) async-start(f32[8,128,384]{2,1,0:T(8,128)} %bitcast.154), calls=%async_computation.3 | async-start | bytes 3145728 | tf_op jit(solution)/shard_map/all_to_all | solution.py:121
  313.9 7.1 %copy-start.5 = (bf16[16,128,384]{2,1,0:T(8,128)(2,1)S(1)}, bf16[16,128,384]{2,1,0:T(8,128)(2,1)}, u32[]{:S(2)}) copy-start(bf16[16,128,384]{2,1,0:T(8,128)(2,1)} %copy.23) | copy-start | bytes 4718596
  327.6 14.4 %copy-start.8 = (bf16[1,384,1536]{2,1,0:T(8,128)(2,1)S(1)}, bf16[1,384,1536]{2,1,0:T(8,128)(2,1)}, u32[]{:S(2)}) copy-start(bf16[1,384,1536]{2,1,0:T(8,128)(2,1)} %fusion.76) | copy-start | bytes 3538948
  335.8 13.7 %collective-permute-start = (bf16[128,384]{1,0:T(8,128)(2,1)S(1)}, bf16[128,384]{1,0:T(8,128)(2,1)S(1)}, u32[]{:S(2)}, u32[]{:S(2)}) collective-permute-start(bf16[128,384]{1,0:T(8,128)(2,1)S(1)} %get-tuple-element.18), channel_id=1, source_target_pairs={{0,0},{1,8},{2,16},{3,24},{4,32},{5,40},{6,48},{7,56},{8,64},{9,72... | collective-permute-start | bytes 294920 | tf_op jit(solution)/shard_map/ppermute | solution.py:131
  339.4 13.0 %collective-permute-start.1 = (bf16[128,384]{1,0:T(8,128)(2,1)S(1)}, bf16[128,384]{1,0:T(8,128)(2,1)S(1)}, u32[]{:S(2)}, u32[]{:S(2)}) collective-permute-start(bf16[128,384]{1,0:T(8,128)(2,1)S(1)} %get-tuple-element.19), channel_id=1, source_target_pairs={{0,64},{1,72},{2,80},{3,88},{4,96},{5,104},{6,112},{7,120},{8,0},{... | collective-permute-start | bytes 294920 | tf_op jit(solution)/shard_map/ppermute | solution.py:131
  (3 other events, 5.2 us)
Sparse Core Ops, SparseCore 0:
  10.3 59.0 all-gather.2
  71.8 26.0 reduce-scatter.1
  178.3 88.4 all-gather.4
where the time goes:
time: 360 us
  waiting for transfers between devices  147 us (41%)
  blocking collectives  75.3 us (21%)
  matrix products  65.7 us (18%)
  starting transfers between devices  30.8 us (9%)
  between operations  14.8 us (4%)
  other arithmetic  14.5 us (4%)
  local copies, waits for them, and re-layouts  11.9 us (3%)
    all_to_all x1, blocking collectives, shards(): lax.all_to_all(result, CHIPS, split_axis=0, concat_axis=0, tiled=True)  75.3 us
    all_gather x1, waiting for transfers between devices, shards(): packed = lax.all_gather(packed, DP, axis=0, tiled=True)  45.7 us
    dot_general x10, matrix products, contract_cols(): lax.dot_general(left_op, right_op, (((1,), (1,)), ((), ())), preferred_el...  34 us
    dot_general x6, matrix products, contract_rows(): lax.dot_general(left_op, right_op, (((0,), (0,)), ((), ())), preferred_el...  31.7 us
    all_to_all x1, waiting for transfers between devices, shards(): lax.all_to_all(out_grad, DP, split_axis=1, concat_axis=0, tiled=True)  30.3 us
    reduce_scatter x1, waiting for transfers between devices, shards(): lax.psum_scatter(result.reshape(2, row_count // 2, ff), 'core', scatter_d...  28.4 us
    all_to_all x1, waiting for transfers between devices, shards(): lax.all_to_all(rows_in, DP, split_axis=1, concat_axis=0, tiled=True)  18.7 us
    all_to_all x2, starting transfers between devices, shards(): lax.all_to_all(partial_rows.reshape(N_TP, rows_dev, width), TP, split_axi...  12.2 us
  transfers between devices with their start and end apart: 9, of which 9 were waited for; matrix products, arithmetic and copies ran while one was open for 19% of the time, Pallas kernels for 0%

commit v1 on v0

--- a/solution.py
+++ b/solution.py
@@ -90,7 +90,9 @@
         hidden_grad * up_vals * sigmoid * (1.0 + gate_vals * (1.0 - sigmoid)) * row_mask
     ).astype(jnp.bfloat16)
     packed = jnp.stack([gate_grad, up_grad], axis=1)
-    packed = lax.all_gather(packed, DP, axis=0, tiled=True)
+    packed = jnp.concatenate(
+        lax.all_to_all(jnp.stack([packed] * lax.axis_size(DP)), DP, 0, 0), axis=0
+    )
     gate_g, up_g = (packed[:, 0], packed[:, 1])
     down_terms = []
     gate_terms = []

time: 360 us -> 534 us (1.48)
  the two profiles are of different devices: /device:TPU:3 before, /device:TPU:12 now
where the time goes in v1:
time: 534 us; the launch traced here: 526 us
  waiting for transfers between devices  297 us (56%)
  blocking collectives  74.7 us (14%)
  matrix products  66.2 us (12%)
  starting transfers between devices  32.3 us (6%)
  local copies, waits for them, and re-layouts  22.1 us (4%)
  other arithmetic  18.1 us (3%)
  between operations  15.4 us (3%)
    all_to_all x1, waiting for transfers between devices, shards(): lax.all_to_all(jnp.stack([packed] * lax.axis_size(DP)), DP, 0, 0)  186 us
    all_to_all x1, blocking collectives, shards(): lax.all_to_all(result, CHIPS, split_axis=0, concat_axis=0, tiled=True)  74.7 us
    dot_general x10, matrix products, contract_cols(): lax.dot_general(left_op, right_op, (((1,), (1,)), ((), ())), preferred_el...  33.4 us
    dot_general x6, matrix products, contract_rows(): lax.dot_general(left_op, right_op, (((0,), (0,)), ((), ())), preferred_el...  32.8 us
    all_to_all x1, waiting for transfers between devices, shards(): lax.all_to_all(out_grad, DP, split_axis=1, concat_axis=0, tiled=True)  30 us
    reduce_scatter x1, waiting for transfers between devices, shards(): lax.psum_scatter(result.reshape(2, row_count // 2, ff), 'core', scatter_d...  29.2 us
    all_to_all x2, waiting for transfers between devices, shards(): lax.all_to_all(partial_rows.reshape(N_TP, rows_dev, width), TP, split_axi...  19.6 us
    all_to_all x1, waiting for transfers between devices, shards(): lax.all_to_all(rows_in, DP, split_axis=1, concat_axis=0, tiled=True)  17.7 us
  transfers between devices with their start and end apart: 9, of which 9 were waited for; matrix products, arithmetic and copies ran while one was open for 12% of the time, Pallas kernels for 0%

profile of v1, /device:TPU:12, one launch (start us, length us, event | category | flops | bytes accessed | tf_op | source)
XLA Modules:
  0.0 525.8 jit_solution(10121381865216121143)
XLA Ops:
  11.7 5.9 %all-to-all-start = ((bf16[128,16,384]{0,2,1:T(8,128)(2,1)}), bf16[128,16,384]{0,2,1:T(8,128)(2,1)S(1)}, u32[]{:S(2)}, u32[]{:S(2)}) async-start(bf16[128,16,384]{0,2,1:T(8,128)(2,1)} %bitcast.1), calls=%async_computation | async-start | bytes 3145728 | tf_op jit(solution)/shard_map/all_to_all | solution.py:63
  18.8 30.0 %all-to-all-done = bf16[128,16,384]{0,2,1:T(8,128)(2,1)S(1)} async-done(((bf16[128,16,384]{0,2,1:T(8,128)(2,1)}), bf16[128,16,384]{0,2,1:T(8,128)(2,1)S(1)}, u32[]{:S(2)}, u32[]{:S(2)}) %all-to-all-start) | async-done | bytes 1572896 | tf_op jit(solution)/shard_map/all_to_all | solution.py:63
  55.4 6.7 %convolution_add_fusion = f32[2048,1536]{1,0:T(8,128)} fusion(f32[2048,1536]{1,0:T(8,128)S(1)} %fusion.115, bf16[2048,384]{1,0:T(8,128)(2,1)S(1)} %bitcast.155, bf16[2,1536,384]{2,1,0:T(8,128)(2,1)S(1)} %copy-done.2), kind=kOutput, calls=%fused_computation.1 | convolution fusion | flops 2419064832 | bytes 27918336 | tf_op jit(solution)/shard_map/dot_general | solution.py:42
  62.1 6.1 %all-gather.2.cloned.1.call-done = bf16[2048,1536]{1,0:T(8,128)(2,1)} async-done(((bf16[128,1536]{1,0:T(8,128)(2,1)}), bf16[2048,1536]{1,0:T(8,128)(2,1)}) %all-gather.2.cloned.1.call-update) | async-done | bytes 6291472 | tf_op jit(solution)/shard_map/all_gather | solution.py:75
  68.1 29.2 %reduce-scatter.2.cloned.1.call-done = f32[1,1024,1536]{2,1,0:T(8,128)} async-done(((f32[2,1024,1536]{2,1,0:T(8,128)}), f32[1,1024,1536]{2,1,0:T(8,128)}) %reduce-scatter.2.cloned.1.call-update) | async-done | bytes 6291472 | tf_op jit(solution)/shard_map/reduce_scatter | solution.py:81
  97.4 74.7 %all_to_all.58 = f32[8,128,1536]{2,1,0:T(8,128)} all-to-all(f32[8,128,1536]{2,1,0:T(8,128)} %bitcast.157), channel_id=1, replica_groups=mesh['x'=4,'ylo'=2,'core'=2,'z'=4,'yhi'=2] {'x','ylo'}, dimensions={0} | all-to-all | bytes 12582912 | tf_op jit(solution)/shard_map/all_to_all | solution.py:84
  172.1 4.3 reduce_sum.27
  178.0 6.9 %all-to-all-start.5 = ((bf16[128,16,384]{0,2,1:T(8,128)(2,1)}), bf16[128,16,384]{0,2,1:T(8,128)(2,1)S(1)}, u32[]{:S(2)}, u32[]{:S(2)}) async-start(bf16[128,16,384]{0,2,1:T(8,128)(2,1)} %bitcast.37), calls=%async_computation.6 | async-start | bytes 3145728 | tf_op jit(solution)/shard_map/all_to_all | solution.py:87
  187.6 17.7 %all-to-all-done.5 = bf16[128,16,384]{0,2,1:T(8,128)(2,1)S(1)} async-done(((bf16[128,16,384]{0,2,1:T(8,128)(2,1)}), bf16[128,16,384]{0,2,1:T(8,128)(2,1)S(1)}, u32[]{:S(2)}, u32[]{:S(2)}) %all-to-all-start.5) | async-done | bytes 1572896 | tf_op jit(solution)/shard_map/all_to_all | solution.py:87
  205.3 7.1 %stack.76 = bf16[16,128,2,1536]{3,1,2,0:T(8,128)(2,1)} broadcast(bf16[128,2,1536]{2,0,1:T(8,128)(2,1)} %pad_maximum_fusion.3), dimensions={1,2,3} | broadcast | bytes 13369344 | tf_op jit(solution)/shard_map/stack | solution.py:94
  212.4 7.2 %all-to-all-start.2 = ((bf16[16,128,2,1536]{3,1,2,0:T(8,128)(2,1)}), bf16[16,128,2,1536]{3,1,2,0:T(8,128)(2,1)}, u32[]{:S(2)}, u32[]{:S(2)}) async-start(bf16[16,128,2,1536]{3,1,2,0:T(8,128)(2,1)} %stack.76), calls=%async_computation.3 | async-start | bytes 25165824 | tf_op jit(solution)/shard_map/all_to_all | solution.py:94
  220.2 6.4 %fusion.88 = bf16[1,1536,384]{2,1,0:T(8,128)(2,1)S(1)} fusion(bf16[2048,384]{1,0:T(8,128)(2,1)S(1)} %bitcast.161, bf16[2048,1536]{1,0:T(8,128)(2,1)} %all-gather.2.cloned.1.call-done, bf16[2048]{0:T(1024)(128)(2,1)S(1)} %broadcast_bitcast_fusion), kind=kOutput, calls=%fused_computation.70 | convolution fusion | flops 2419654656 | bytes 9048064 | tf_op jit(solution)/shard_map/dot_general | solution.py:36
  226.5 6.3 %fusion.91 = bf16[1,1536,384]{2,1,0:T(8,128)(2,1)S(1)} fusion(bf16[2048,384]{1,0:T(8,128)(2,1)S(1)} %bitcast.162, bf16[2048,1536]{1,0:T(8,128)(2,1)} %all-gather.2.cloned.1.call-done, bf16[2048]{0:T(1024)(128)(2,1)S(1)} %broadcast_bitcast_fusion.1), kind=kOutput, calls=%fused_computation.71 | convolution fusion | flops 2419654656 | bytes 9048064 | tf_op jit(solution)/shard_map/dot_general | solution.py:36
  235.4 185.7 %all-to-all-done.2 = bf16[16,128,2,1536]{3,1,2,0:T(8,128)(2,1)} async-done(((bf16[16,128,2,1536]{3,1,2,0:T(8,128)(2,1)}), bf16[16,128,2,1536]{3,1,2,0:T(8,128)(2,1)}, u32[]{:S(2)}, u32[]{:S(2)}) %all-to-all-start.2) | async-done | bytes 12582944 | tf_op jit(solution)/shard_map/all_to_all | solution.py:94
  421.1 6.6 %copy.32 = bf16[16,128,2,1536]{3,1,0,2:T(8,128)(2,1)S(1)} copy(bf16[16,128,2,1536]{3,1,2,0:T(8,128)(2,1)} %all-to-all-done.2) | data formatting | bytes 25165824 | tf_op jit(solution)/shard_map/all_to_all | solution.py:94
  430.5 3.7 fusion.85
  448.8 6.7 %all-to-all-start.4 = ((f32[8,128,384]{2,1,0:T(8,128)}), f32[8,128,384]{2,1,0:T(8,128)S(1)}, u32[]{:S(2)}, u32[]{:S(2)}) async-start(f32[8,128,384]{2,1,0:T(8,128)} %bitcast.33), calls=%async_computation.5 | async-start | bytes 3145728 | tf_op jit(solution)/shard_map/all_to_all | solution.py:123
  458.5 3.9 fusion.28
  462.4 4.9 add_add_fusion.1
  467.3 11.2 %all-to-all-done.4 = f32[8,128,384]{2,1,0:T(8,128)S(1)} async-done(((f32[8,128,384]{2,1,0:T(8,128)}), f32[8,128,384]{2,1,0:T(8,128)S(1)}, u32[]{:S(2)}, u32[]{:S(2)}) %all-to-all-start.4) | async-done | bytes 1572896 | tf_op jit(solution)/shard_map/all_to_all | solution.py:123
  482.2 7.1 %fusion.76 = bf16[1,384,1536]{2,1,0:T(8,128)(2,1)} fusion(bf16[2048,384]{1,0:T(8,128)(2,1)} %bitcast.165, bf16[2048,2,1536]{2,0,1:T(8,128)(2,1)} %bitcast.153, bf16[2048]{0:T(1024)(128)(2,1)S(1)} %broadcast_bitcast_fusion), kind=kOutput, calls=%fused_computation.66 | convolution fusion | flops 2419654656 | bytes 9048064 | tf_op jit(solution)/shard_map/dot_general | solution.py:36
  489.3 6.5 %fusion.79 = bf16[1,384,1536]{2,1,0:T(8,128)(2,1)} fusion(bf16[2048,384]{1,0:T(8,128)(2,1)S(1)} %bitcast.166, bf16[2048,2,1536]{2,0,1:T(8,128)(2,1)} %bitcast.154, bf16[2048]{0:T(1024)(128)(2,1)S(1)} %broadcast_bitcast_fusion.1), kind=kOutput, calls=%fused_computation.67 | convolution fusion | flops 2419654656 | bytes 9048064 | tf_op jit(solution)/shard_map/dot_general | solution.py:36
  495.9 8.4 %all-to-all-done.3 = f32[8,128,384]{2,1,0:T(8,128)S(1)} async-done(((f32[8,128,384]{2,1,0:T(8,128)}), f32[8,128,384]{2,1,0:T(8,128)S(1)}, u32[]{:S(2)}, u32[]{:S(2)}) %all-to-all-start.3) | async-done | bytes 1572896 | tf_op jit(solution)/shard_map/all_to_all | solution.py:123
  509.4 7.5 %collective-permute-done = bf16[128,384]{1,0:T(8,128)(2,1)S(1)} collective-permute-done((bf16[128,384]{1,0:T(8,128)(2,1)S(1)}, bf16[128,384]{1,0:T(8,128)(2,1)S(1)}, u32[]{:S(2)}, u32[]{:S(2)}) %collective-permute-start) | collective-permute-done | bytes 98336 | tf_op jit(solution)/shard_map/ppermute | solution.py:133
  (82 shorter events, 49.7 us)
Async XLA Ops:
  7.2 3.0 copy-start.3
  7.2 60.9 %all-gather.2.cloned.1.call-start = ((), (), s32[]{:S(2)}) async-start(), calls=%async_computation.7 | async-start | bytes 6684672 | tf_op jit(solution)/shard_map/all_gather | solution.py:75
  11.7 5.9 %copy-start.9 = (s32[16]{0:T(128)S(1)}, s32[16]{0:T(128)}, u32[]{:S(2)}) copy-start(s32[16]{0:T(128)} %constant.55) | copy-start | bytes 196
  11.7 5.9 %copy-start = (s32[16]{0:T(128)S(1)}, s32[16]{0:T(128)}, u32[]{:S(2)}) copy-start(s32[16]{0:T(128)} %param.18) | copy-start | bytes 196
  11.7 37.1 %all-to-all-start = ((bf16[128,16,384]{0,2,1:T(8,128)(2,1)}), bf16[128,16,384]{0,2,1:T(8,128)(2,1)S(1)}, u32[]{:S(2)}, u32[]{:S(2)}) async-start(bf16[128,16,384]{0,2,1:T(8,128)(2,1)} %bitcast.1), calls=%async_computation | async-start | bytes 3145728 | tf_op jit(solution)/shard_map/all_to_all | solution.py:63
  17.6 79.8 %reduce-scatter.2.cloned.1.call-start = ((), (), s32[]{:S(2)}) async-start(), calls=%async_computation.8 | async-start | bytes 18874368 | tf_op jit(solution)/shard_map/reduce_scatter | solution.py:81
  172.1 4.4 copy-start.4
  178.0 6.9 %copy-start.7 = (bf16[128,1536]{1,0:T(8,128)(2,1)S(1)}, bf16[128,1536]{1,0:T(8,128)(2,1)}, u32[]{:S(2)}) copy-start(bf16[128,1536]{1,0:T(8,128)(2,1)} %param.12) | copy-start | bytes 1179652
  178.0 27.3 %all-to-all-start.5 = ((bf16[128,16,384]{0,2,1:T(8,128)(2,1)}), bf16[128,16,384]{0,2,1:T(8,128)(2,1)S(1)}, u32[]{:S(2)}, u32[]{:S(2)}) async-start(bf16[128,16,384]{0,2,1:T(8,128)(2,1)} %bitcast.37), calls=%async_computation.6 | async-start | bytes 3145728 | tf_op jit(solution)/shard_map/all_to_all | solution.py:87
  212.4 208.7 %all-to-all-start.2 = ((bf16[16,128,2,1536]{3,1,2,0:T(8,128)(2,1)}), bf16[16,128,2,1536]{3,1,2,0:T(8,128)(2,1)}, u32[]{:S(2)}, u32[]{:S(2)}) async-start(bf16[16,128,2,1536]{3,1,2,0:T(8,128)(2,1)} %stack.76), calls=%async_computation.3 | async-start | bytes 25165824 | tf_op jit(solution)/shard_map/all_to_all | solution.py:94
  235.4 195.0 %copy-start.5 = (bf16[16,128,384]{2,1,0:T(8,128)(2,1)}, bf16[16,128,384]{2,1,0:T(8,128)(2,1)S(1)}, u32[]{:S(2)}) copy-start(bf16[16,128,384]{2,1,0:T(8,128)(2,1)S(1)} %copy.34) | copy-start | bytes 4718596
  427.7 18.0 %copy-start.1 = (bf16[16,128,2,1536]{3,1,0,2:T(8,128)(2,1)}, bf16[16,128,2,1536]{3,1,0,2:T(8,128)(2,1)S(1)}, u32[]{:S(2)}) copy-start(bf16[16,128,2,1536]{3,1,0,2:T(8,128)(2,1)S(1)} %copy.32) | copy-start | bytes 37748740
  430.5 3.8 copy-start.10
  434.2 1.8 copy-start.12
  448.8 29.8 %all-to-all-start.4 = ((f32[8,128,384]{2,1,0:T(8,128)}), f32[8,128,384]{2,1,0:T(8,128)S(1)}, u32[]{:S(2)}, u32[]{:S(2)}) async-start(f32[8,128,384]{2,1,0:T(8,128)} %bitcast.33), calls=%async_computation.5 | async-start | bytes 3145728 | tf_op jit(solution)/shard_map/all_to_all | solution.py:123
  455.5 3.1 copy-start.11
  458.5 3.9 copy-start.13
  458.5 3.9 copy-start.14
  458.5 3.9 copy-start.15
  478.6 25.7 %all-to-all-start.3 = ((f32[8,128,384]{2,1,0:T(8,128)}), f32[8,128,384]{2,1,0:T(8,128)S(1)}, u32[]{:S(2)}, u32[]{:S(2)}) async-start(f32[8,128,384]{2,1,0:T(8,128)} %bitcast.167), calls=%async_computation.4 | async-start | bytes 3145728 | tf_op jit(solution)/shard_map/all_to_all | solution.py:123
  482.1 7.1 %copy-start.6 = (bf16[16,128,384]{2,1,0:T(8,128)(2,1)S(1)}, bf16[16,128,384]{2,1,0:T(8,128)(2,1)}, u32[]{:S(2)}) copy-start(bf16[16,128,384]{2,1,0:T(8,128)(2,1)} %copy-done.5) | copy-start | bytes 4718596
  495.9 10.6 %copy-start.8 = (bf16[1,384,1536]{2,1,0:T(8,128)(2,1)S(1)}, bf16[1,384,1536]{2,1,0:T(8,128)(2,1)}, u32[]{:S(2)}) copy-start(bf16[1,384,1536]{2,1,0:T(8,128)(2,1)} %fusion.76) | copy-start | bytes 3538948
  504.5 12.4 %collective-permute-start = (bf16[128,384]{1,0:T(8,128)(2,1)S(1)}, bf16[128,384]{1,0:T(8,128)(2,1)S(1)}, u32[]{:S(2)}, u32[]{:S(2)}) collective-permute-start(bf16[128,384]{1,0:T(8,128)(2,1)S(1)} %get-tuple-element.18), channel_id=1, source_target_pairs={{0,0},{1,8},{2,16},{3,24},{4,32},{5,40},{6,48},{7,56},{8,64},{9,72... | collective-permute-start | bytes 294920 | tf_op jit(solution)/shard_map/ppermute | solution.py:133
  506.4 11.6 %collective-permute-start.1 = (bf16[128,384]{1,0:T(8,128)(2,1)S(1)}, bf16[128,384]{1,0:T(8,128)(2,1)S(1)}, u32[]{:S(2)}, u32[]{:S(2)}) collective-permute-start(bf16[128,384]{1,0:T(8,128)(2,1)S(1)} %get-tuple-element.19), channel_id=1, source_target_pairs={{0,64},{1,72},{2,80},{3,88},{4,96},{5,104},{6,112},{7,120},{8,0},{... | collective-permute-start | bytes 294920 | tf_op jit(solution)/shard_map/ppermute | solution.py:133
  (1 other events, 1.7 us)
Sparse Core Ops, SparseCore 0:
  10.3 57.7 all-gather.1
  70.5 26.7 reduce-scatter.1
